TPU v7x, 32 devices: a whole 2x2x4 slice. The times are simulated.
32 devices in a mesh: section: 4 (over z), dp: 8 (over y, x, core).
Axes of the slice: x: 2, y: 2, z: 4, core: 2. Of those that a mesh axis runs over, the one named last changes fastest.
Arguments:
- layer_inputs: bfloat16 [4, 8, 128, 2560], P('section', 'dp'), may hold values from -6 to 6
- w_bc: bfloat16 [4, 2560, 256], P('section'), may hold values from -0.125 to 0.125
- log_decay: float32 [4, 8, 128, 40], P('section', 'dp'), may hold values from -1.7 to 0, as said below
- top_grad: bfloat16 [8, 128, 2560], P('dp'), may hold values from -6 to 6
Outputs:
- grad_inputs: bfloat16 [4, 8, 128, 2560], P('section', 'dp')
- grad_w: float32 [4, 2560, 256], P('section', 'dp')
Inputs may be any that keep to these rules, and one draw needn't show every extreme that they name: `log_decay`: every entry is negative.
All inputs are finite; a program needn't handle non-finite values.
Results may differ from a plain program's by a relative error of at most 0.0085.
Values may be sent and summed in bfloat16 or wider, within the bound.
No kernel may reach another device: no remote copies, remote signals or barrier semaphores. Data moves between devices by JAX's collectives and lax.ppermute only.
A program may use at most 64 MiB of HBM per device.

v0:
```python
import jax
import jax.numpy as jnp
from jax import lax
from jax.sharding import PartitionSpec as P

MICRO = 4


def shortened(value):
    return jax.tree.map(lambda a: a.astype(jnp.bfloat16) if a.dtype == jnp.float32 else a, value)


def passed_along(block, axis, distance):
    devices = range(lax.axis_size(axis))
    route = [(i - distance, i) for i in devices if i - distance in devices]
    return lax.ppermute(block, axis, route)


def block_terms(inputs_b, in_b, out_b, rates, grads_b, carried, state_in, factor):
    length = inputs_b.shape[0]
    cumulative = jnp.cumsum(rates, axis=0)
    ending = cumulative[-1]
    locations = jnp.arange(length)
    lower_mask = (locations[:, None] >= locations[None, :])[:, :, None]
    spread = jnp.where(lower_mask, cumulative[:, None, :] - cumulative[None, :, :], 0.0)
    decays = jnp.where(lower_mask, jnp.exp(spread), 0.0)
    tail_decay = jnp.exp(ending[None, :] - cumulative)
    leading = jnp.exp(cumulative)
    scores = jnp.dot(out_b, in_b.T, preferred_element_type=jnp.float32)
    weighted = (factor * decays * scores[:, :, None]).astype(jnp.bfloat16)
    carried_b = carried.astype(jnp.bfloat16)
    state_b = state_in.astype(jnp.bfloat16)
    grad_feats = jnp.einsum("kjh,khp->jhp", weighted, grads_b, preferred_element_type=jnp.float32)
    grad_feats = grad_feats + tail_decay[:, :, None] * jnp.einsum(
        "hpn,jn->jhp", carried_b, in_b, preferred_element_type=jnp.float32
    )
    pair_dots = jnp.einsum("khp,jhp->kjh", grads_b, inputs_b, preferred_element_type=jnp.float32)
    mixing = jnp.sum(decays * pair_dots, axis=2).astype(jnp.bfloat16)
    tail_inputs = (tail_decay[:, :, None] * inputs_b.astype(jnp.float32)).astype(jnp.bfloat16)
    lead_grads = (leading[:, :, None] * grads_b.astype(jnp.float32)).astype(jnp.bfloat16)
    grad_inmap = factor * jnp.dot(mixing.T, out_b, preferred_element_type=jnp.float32)
    grad_inmap = grad_inmap + jnp.einsum(
        "jhp,hpn->jn", tail_inputs, carried_b, preferred_element_type=jnp.float32
    )
    grad_outmap = factor * (
        jnp.dot(mixing, in_b, preferred_element_type=jnp.float32)
        + jnp.einsum("ihp,hpn->in", lead_grads, state_b, preferred_element_type=jnp.float32)
    )
    carry_out = factor * jnp.einsum(
        "khp,kn->hpn", lead_grads, out_b, preferred_element_type=jnp.float32
    )
    carry_out = carry_out + jnp.exp(ending)[:, None, None] * carried
    return (grad_feats, grad_inmap, grad_outmap, carry_out)


def block_end(inputs_b, in_b, rates, state_in):
    cumulative = jnp.cumsum(rates, axis=0)
    ending = cumulative[-1]
    tail_decay = jnp.exp(ending[None, :] - cumulative)
    tail_inputs = (tail_decay[:, :, None] * inputs_b.astype(jnp.float32)).astype(jnp.bfloat16)
    fresh = jnp.einsum("jhp,jn->hpn", tail_inputs, in_b, preferred_element_type=jnp.float32)
    return jnp.exp(ending)[:, None, None] * state_in + fresh


def split_block(inputs_c, map_block, head_count):
    length, features = inputs_c.shape
    state_size = map_block.shape[1] // 2
    inputs_b = inputs_c.reshape(length, head_count, features // head_count)
    in_b = map_block[:, :state_size]
    out_b = map_block[:, state_size:]
    return (inputs_b, in_b, out_b)


def block_back(inputs_c, map_block, rates, grads_c, carried, state_in, weights):
    length, features = inputs_c.shape
    head_count = rates.shape[1]
    factor = 0.25 / (map_block.shape[1] // 2)
    inputs_b, in_b, out_b = split_block(inputs_c, map_block, head_count)
    grads_b = grads_c.reshape(length, head_count, features // head_count)
    grad_feats, grad_inmap, grad_outmap, carry_out = block_terms(
        inputs_b, in_b, out_b, rates, grads_b, carried, state_in, factor
    )
    grad_bc = jnp.concatenate([grad_inmap, grad_outmap], axis=1).astype(jnp.bfloat16)
    back_proj = lax.dot_general(
        grad_bc, weights, (((1,), (1,)), ((), ())), preferred_element_type=jnp.float32
    )
    summed = grads_c.astype(jnp.float32) + grad_feats.reshape(length, features) + back_proj
    return (summed.astype(jnp.bfloat16), carry_out, grad_bc)


def layer_starts(inputs_s, bc_s, rates_s):
    head_count = rates_s.shape[1]
    features = inputs_s.shape[1]
    state_size = bc_s.shape[1] // 2
    block_len = inputs_s.shape[0] // MICRO
    state_now = jnp.zeros((head_count, features // head_count, state_size), jnp.float32)
    saved = []
    for block_no in range(MICRO):
        lo_row = block_no * block_len
        inputs_b, in_b, out_b = split_block(
            inputs_s[lo_row : lo_row + block_len], bc_s[lo_row : lo_row + block_len], head_count
        )
        saved.append(state_now)
        state_now = block_end(inputs_b, in_b, rates_s[lo_row : lo_row + block_len], state_now)
    return jnp.stack(saved)


def shards(layer_inputs, w_bc, log_decay, top_grad):
    sections = lax.axis_size("section")
    section_id = lax.axis_index("section")
    lay_dev, seq_dev, tok_len, features = layer_inputs.shape
    block_len = tok_len // MICRO
    bc_all = jnp.einsum(
        "lstd,ldc->lstc", layer_inputs, w_bc, preferred_element_type=jnp.float32
    ).astype(jnp.bfloat16)
    starts = jax.vmap(jax.vmap(layer_starts))(layer_inputs, bc_all, log_decay)
    is_top = section_id == sections - 1
    back_all = jax.vmap(block_back, in_axes=(0, 0, 0, 0, 0, 0, None))

    def advance(counter, loop_state):
        incoming, carried, grad_store, map_store = loop_state
        offset = counter - (sections - 1 - section_id)
        is_valid = (offset >= 0) & (offset < MICRO)
        block_no = jnp.clip(MICRO - 1 - offset, 0, MICRO - 1)
        row_start = block_no * block_len
        from_top = lax.dynamic_slice_in_dim(top_grad, row_start, block_len, 1)
        grad_block = jnp.where(is_top, from_top, incoming)

        def compute(stores):
            carried_in, grads_in, maps_in = stores
            current = grad_block
            for level_no in reversed(range(lay_dev)):
                inputs_c = lax.dynamic_slice_in_dim(layer_inputs[level_no], row_start, block_len, 1)
                map_block = lax.dynamic_slice_in_dim(bc_all[level_no], row_start, block_len, 1)
                rates = lax.dynamic_slice_in_dim(log_decay[level_no], row_start, block_len, 1)
                state_in = lax.dynamic_index_in_dim(starts[level_no], block_no, 1, keepdims=False)
                level_grads, carry_out, grad_bc = back_all(
                    inputs_c,
                    map_block,
                    rates,
                    current,
                    carried_in[level_no],
                    state_in,
                    w_bc[level_no],
                )
                carried_in = carried_in.at[level_no].set(carry_out)
                grads_in = grads_in.at[level_no].set(
                    lax.dynamic_update_slice_in_dim(grads_in[level_no], level_grads, row_start, 1)
                )
                maps_in = maps_in.at[level_no].set(
                    lax.dynamic_update_slice_in_dim(maps_in[level_no], grad_bc, row_start, 1)
                )
                current = level_grads
            return (current, (carried_in, grads_in, maps_in))

        def passing(stores):
            return (jnp.zeros_like(grad_block), stores)

        outgoing, updated = lax.cond(is_valid, compute, passing, (carried, grad_store, map_store))
        received = jax.tree.map(
            lambda part, own: part.astype(own.dtype),
            passed_along(shortened(outgoing), "section", -1),
            outgoing,
        )
        return (received, updated[0], updated[1], updated[2])

    initial = (
        jnp.zeros((seq_dev, block_len, features), jnp.bfloat16),
        jnp.zeros((lay_dev,) + starts.shape[1:2] + starts.shape[3:], jnp.float32),
        jnp.zeros(layer_inputs.shape, jnp.bfloat16),
        jnp.zeros(bc_all.shape, jnp.bfloat16),
    )
    final_state = lax.fori_loop(0, MICRO + sections - 1, advance, initial)
    grad_inputs = final_state[2]
    map_store = final_state[3]
    ways = lax.axis_size("dp")
    divisor = ways * seq_dev
    rows_here = layer_inputs.reshape(lay_dev, seq_dev * tok_len, features)
    rows_all = lax.all_to_all(rows_here, "dp", 2, 1, tiled=True)
    maps_here = map_store.reshape(lay_dev, seq_dev * tok_len, map_store.shape[-1])
    maps_all = lax.all_gather(maps_here, "dp", axis=1, tiled=True)
    grad_w = (
        jnp.einsum("lrd,lrc->ldc", rows_all, maps_all, preferred_element_type=jnp.float32) / divisor
    )
    return (grad_inputs, grad_w)


def solution(mesh):
    in_specs = (
        P("section", "dp", None, None),
        P("section", None, None),
        P("section", "dp", None, None),
        P("dp", None, None),
    )
    out_specs = (P("section", "dp", None, None), P("section", "dp", None))
    return jax.shard_map(shards, mesh=mesh, in_specs=in_specs, out_specs=out_specs, check_vma=False)
```

profile of v0, /device:TPU:0, one launch (start us, length us, event | category | flops | bytes accessed | tf_op | source)
XLA Modules:
  0.0 188.5 jit_solution(8316372705247162726)
XLA Ops:
  0.6 2.5 %copy.89 = bf16[1,128,2560]{1,0,2:T(2,128)(2,1)S(1)} copy(bf16[1,128,2560]{2,1,0:T(8,128)(2,1)} %bitcast.43) | data formatting | bytes 1310720 | tf_op jit(solution)/shard_map/reshape | solution.py:178
  3.7 14.3 %reduce.10 = bf16[2560,128]{1,0:T(8,128)(2,1)S(1)} reduce(bf16[2560,1,128]{2,1,0:T(2,128)(2,1)S(1)} %bitcast.178, bf16[]{:T(256)} %broadcast.353), dimensions={1}, to_apply=%bitcast.170.reduce_sub_computation | reduce | bytes 1310722
  18.9 5.2 %all-to-all-start = ((bf16[8,2,20480]{2,1,0:T(2,128)(2,1)}), bf16[8,2,20480]{2,1,0:T(2,128)(2,1)}, u32[]{:S(2)}, u32[]{:S(2)}) async-start(bf16[8,2,20480]{2,1,0:T(2,128)(2,1)} %reshape.676), calls=%async_computation | async-start | bytes 1310720 | tf_op jit(solution)/shard_map/all_to_all | solution.py:179
  28.2 1.4 fusion.61
  31.3 1.9 %pad_maximum_fusion = bf16[1,1,4,40,64,128]{5,4,3,2,1,0:T(8,128)(2,1)} fusion(bf16[1,1,1,40,64,128]{5,4,3,2,1,0:T(8,128)(2,1)S(1)} %fusion.54, f32[1,1,1,40,64,128]{5,4,3,2,1,0:T(8,128)S(1)} %bitcast.177, f32[1,1,1,40,64,128]{5,4,3,2,1,0:T(8,128)S(1)} %bitcast.176, bf16[4]{0:T(256)(128)(2,1)S(1)} %pad.10.clone), kind=kLoop, calls=%fused_computation.78 | loop fusion | flops 3932160 | bytes 5898248 | tf_op jit(solution)/shard_map/vmap(vmap())/stack | solution.py:105
  34.9 139.4 %while.24 = (s32[]{:T(128)}, bf16[1,32,2560]{2,1,0:T(8,128)(2,1)S(1)}, f32[1,1,40,64,128]{4,3,2,1,0:T(8,128)S(1)}, bf16[1,1,128,2560]{3,2,1,0:T(8,128)(2,1)}, bf...) while((s32[]{:T(128)}, ...), condition=%wide.region_8.9_spmd, body=%wide.region_3.8_spmd.sunk | while | flops 140346368 | bytes 17553168 | solution.py:173
  36.3 7.4 %collective-permute-done = bf16[1,32,2560]{2,1,0:T(8,128)(2,1)S(1)} collective-permute-done((bf16[1,32,2560]{2,1,0:T(8,128)(2,1)S(1)}, bf16[1,32,2560]{2,1,0:T(8,128)(2,1)S(1)}, u32[]{:S(2)}, u32[]{:S(2)}) %collective-permute-start) | collective-permute-done | bytes 163872 | tf_op jit(solution)/shard_map/while/body/eval_jaxpr/ppermute | solution.py:16
  45.0 6.4 %collective-permute-done = bf16[1,32,2560]{2,1,0:T(8,128)(2,1)S(1)} collective-permute-done((bf16[1,32,2560]{2,1,0:T(8,128)(2,1)S(1)}, bf16[1,32,2560]{2,1,0:T(8,128)(2,1)S(1)}, u32[]{:S(2)}, u32[]{:S(2)}) %collective-permute-start) | collective-permute-done | bytes 163872 | tf_op jit(solution)/shard_map/while/body/eval_jaxpr/ppermute | solution.py:16
  52.7 42.5 %collective-permute-done = bf16[1,32,2560]{2,1,0:T(8,128)(2,1)S(1)} collective-permute-done((bf16[1,32,2560]{2,1,0:T(8,128)(2,1)S(1)}, bf16[1,32,2560]{2,1,0:T(8,128)(2,1)S(1)}, u32[]{:S(2)}, u32[]{:S(2)}) %collective-permute-start) | collective-permute-done | bytes 163872 | tf_op jit(solution)/shard_map/while/body/eval_jaxpr/ppermute | solution.py:16
  95.2 12.6 %conditional.2 = (bf16[1,32,2560]{2,1,0:T(8,128)(2,1)S(1)}, f32[1,1,40,64,128]{4,3,2,1,0:T(8,128)S(1)}, bf16[1,1,128,2560]{3,2,1,0:T(8,128)(2,1)}, bf16[1,1,128,256]{3,2,1,0:T(8,128)(2,1)}) conditional(s32[]{:T(128)} %convert_element_type.236, (f32[1,1,40,64,128]{4,3,2,1,0:T(8,128)S(1)}, bf16[1,1,128,2560]{3,2,1,0:T(8,128)(2,1)}, ...), branch_computations={%region_4.4_spmd, %region_5.7_spmd} | conditional | flops 140346368 | bytes 16897460 | solution.py:159
  104.6 2.5 %bitcast_dynamic-update-slice_fusion = (bf16[1,1,128,2560]{3,2,1,0:T(8,128)(2,1)}, bf16[1,32,2560]{2,1,0:T(8,128)(2,1)S(1)}) fusion(bf16[1,1,128,2560]{3,2,1,0:T(8,128)(2,1)} %get-tuple-element.483, s32[]{:T(128)S(6)} %select_n.90, bf16[1,2560,256]{2,1,0:T(8,128)(2,1)} %get-tuple-element.482, bf16[32,128]{1,0:T(8,128)(2,1)S(1)} %fusion.13, ...), kind=kOutput, calls=%fused_computation.46 | convolution fusion | flops 42303488 | bytes 2146308 | tf_op jit(solution)/shard_map/while/body/eval_jaxpr/cond/branch_1_fun/vmap()/dot_general | solution.py:84
  109.1 5.9 %collective-permute-done = bf16[1,32,2560]{2,1,0:T(8,128)(2,1)S(1)} collective-permute-done((bf16[1,32,2560]{2,1,0:T(8,128)(2,1)S(1)}, bf16[1,32,2560]{2,1,0:T(8,128)(2,1)S(1)}, u32[]{:S(2)}, u32[]{:S(2)}) %collective-permute-start) | collective-permute-done | bytes 163872 | tf_op jit(solution)/shard_map/while/body/eval_jaxpr/ppermute | solution.py:16
  115.0 12.6 %conditional.2 = (bf16[1,32,2560]{2,1,0:T(8,128)(2,1)S(1)}, f32[1,1,40,64,128]{4,3,2,1,0:T(8,128)S(1)}, bf16[1,1,128,2560]{3,2,1,0:T(8,128)(2,1)}, bf16[1,1,128,256]{3,2,1,0:T(8,128)(2,1)}) conditional(s32[]{:T(128)} %convert_element_type.236, (f32[1,1,40,64,128]{4,3,2,1,0:T(8,128)S(1)}, bf16[1,1,128,2560]{3,2,1,0:T(8,128)(2,1)}, ...), branch_computations={%region_4.4_spmd, %region_5.7_spmd} | conditional | flops 140346368 | bytes 16897460 | solution.py:159
  120.4 1.4 fusion.13
  124.4 2.5 %bitcast_dynamic-update-slice_fusion = (bf16[1,1,128,2560]{3,2,1,0:T(8,128)(2,1)}, bf16[1,32,2560]{2,1,0:T(8,128)(2,1)S(1)}) fusion(bf16[1,1,128,2560]{3,2,1,0:T(8,128)(2,1)} %get-tuple-element.483, s32[]{:T(128)S(6)} %select_n.90, bf16[1,2560,256]{2,1,0:T(8,128)(2,1)} %get-tuple-element.482, bf16[32,128]{1,0:T(8,128)(2,1)S(1)} %fusion.13, ...), kind=kOutput, calls=%fused_computation.46 | convolution fusion | flops 42303488 | bytes 2146308 | tf_op jit(solution)/shard_map/while/body/eval_jaxpr/cond/branch_1_fun/vmap()/dot_general | solution.py:84
  128.9 5.9 %collective-permute-done = bf16[1,32,2560]{2,1,0:T(8,128)(2,1)S(1)} collective-permute-done((bf16[1,32,2560]{2,1,0:T(8,128)(2,1)S(1)}, bf16[1,32,2560]{2,1,0:T(8,128)(2,1)S(1)}, u32[]{:S(2)}, u32[]{:S(2)}) %collective-permute-start) | collective-permute-done | bytes 163872 | tf_op jit(solution)/shard_map/while/body/eval_jaxpr/ppermute | solution.py:16
  134.8 12.6 %conditional.2 = (bf16[1,32,2560]{2,1,0:T(8,128)(2,1)S(1)}, f32[1,1,40,64,128]{4,3,2,1,0:T(8,128)S(1)}, bf16[1,1,128,2560]{3,2,1,0:T(8,128)(2,1)}, bf16[1,1,128,256]{3,2,1,0:T(8,128)(2,1)}) conditional(s32[]{:T(128)} %convert_element_type.236, (f32[1,1,40,64,128]{4,3,2,1,0:T(8,128)S(1)}, bf16[1,1,128,2560]{3,2,1,0:T(8,128)(2,1)}, ...), branch_computations={%region_4.4_spmd, %region_5.7_spmd} | conditional | flops 140346368 | bytes 16897460 | solution.py:159
  144.2 2.5 %bitcast_dynamic-update-slice_fusion = (bf16[1,1,128,2560]{3,2,1,0:T(8,128)(2,1)}, bf16[1,32,2560]{2,1,0:T(8,128)(2,1)S(1)}) fusion(bf16[1,1,128,2560]{3,2,1,0:T(8,128)(2,1)} %get-tuple-element.483, s32[]{:T(128)S(6)} %select_n.90, bf16[1,2560,256]{2,1,0:T(8,128)(2,1)} %get-tuple-element.482, bf16[32,128]{1,0:T(8,128)(2,1)S(1)} %fusion.13, ...), kind=kOutput, calls=%fused_computation.46 | convolution fusion | flops 42303488 | bytes 2146308 | tf_op jit(solution)/shard_map/while/body/eval_jaxpr/cond/branch_1_fun/vmap()/dot_general | solution.py:84
  148.7 5.9 %collective-permute-done = bf16[1,32,2560]{2,1,0:T(8,128)(2,1)S(1)} collective-permute-done((bf16[1,32,2560]{2,1,0:T(8,128)(2,1)S(1)}, bf16[1,32,2560]{2,1,0:T(8,128)(2,1)S(1)}, u32[]{:S(2)}, u32[]{:S(2)}) %collective-permute-start) | collective-permute-done | bytes 163872 | tf_op jit(solution)/shard_map/while/body/eval_jaxpr/ppermute | solution.py:16
  154.6 12.6 %conditional.2 = (bf16[1,32,2560]{2,1,0:T(8,128)(2,1)S(1)}, f32[1,1,40,64,128]{4,3,2,1,0:T(8,128)S(1)}, bf16[1,1,128,2560]{3,2,1,0:T(8,128)(2,1)}, bf16[1,1,128,256]{3,2,1,0:T(8,128)(2,1)}) conditional(s32[]{:T(128)} %convert_element_type.236, (f32[1,1,40,64,128]{4,3,2,1,0:T(8,128)S(1)}, bf16[1,1,128,2560]{3,2,1,0:T(8,128)(2,1)}, ...), branch_computations={%region_4.4_spmd, %region_5.7_spmd} | conditional | flops 140346368 | bytes 16897460 | solution.py:159
  164.0 2.5 %bitcast_dynamic-update-slice_fusion = (bf16[1,1,128,2560]{3,2,1,0:T(8,128)(2,1)}, bf16[1,32,2560]{2,1,0:T(8,128)(2,1)S(1)}) fusion(bf16[1,1,128,2560]{3,2,1,0:T(8,128)(2,1)} %get-tuple-element.483, s32[]{:T(128)S(6)} %select_n.90, bf16[1,2560,256]{2,1,0:T(8,128)(2,1)} %get-tuple-element.482, bf16[32,128]{1,0:T(8,128)(2,1)S(1)} %fusion.13, ...), kind=kOutput, calls=%fused_computation.46 | convolution fusion | flops 42303488 | bytes 2146308 | tf_op jit(solution)/shard_map/while/body/eval_jaxpr/cond/branch_1_fun/vmap()/dot_general | solution.py:84
  168.5 5.9 %collective-permute-done = bf16[1,32,2560]{2,1,0:T(8,128)(2,1)S(1)} collective-permute-done((bf16[1,32,2560]{2,1,0:T(8,128)(2,1)S(1)}, bf16[1,32,2560]{2,1,0:T(8,128)(2,1)S(1)}, u32[]{:S(2)}, u32[]{:S(2)}) %collective-permute-start) | collective-permute-done | bytes 163872 | tf_op jit(solution)/shard_map/while/body/eval_jaxpr/ppermute | solution.py:16
  174.4 10.2 %all-gather = bf16[1,1,1024,256]{3,2,1,0:T(8,128)(2,1)S(1)} all-gather(bf16[1,1,128,256]{3,2,1,0:T(8,128)(2,1)} %get-tuple-element.508), channel_id=2, replica_groups=mesh['section'=4,'dp'=8] {'dp'}, dimensions={2}, use_global_device_ids=true | all-gather | bytes 589824 | tf_op jit(solution)/shard_map/all_gather | solution.py:181
  184.6 2.3 %reshape.677 = bf16[2560,1,128]{2,1,0:T(2,128)(2,1)S(1)} reshape(bf16[8,2,20480]{2,1,0:T(2,128)(2,1)} %all-to-all-done) | data formatting | bytes 1310720
  (185 shorter events, 58.0 us)
Async XLA Ops:
  17.9 6.2 %copy-start.1 = (f32[1,1,128,40]{2,3,1,0:T(8,128)S(1)}, f32[1,1,128,40]{2,3,1,0:T(8,128)}, u32[]{:S(2)}) copy-start(f32[1,1,128,40]{2,3,1,0:T(8,128)} %param.16) | copy-start | bytes 61444
  18.9 165.6 %all-to-all-start = ((bf16[8,2,20480]{2,1,0:T(2,128)(2,1)}), bf16[8,2,20480]{2,1,0:T(2,128)(2,1)}, u32[]{:S(2)}, u32[]{:S(2)}) async-start(bf16[8,2,20480]{2,1,0:T(2,128)(2,1)} %reshape.676), calls=%async_computation | async-start | bytes 1310720 | tf_op jit(solution)/shard_map/all_to_all | solution.py:179
  26.7 1.6 copy-start
  35.0 8.7 %collective-permute-start = (bf16[1,32,2560]{2,1,0:T(8,128)(2,1)S(1)}, bf16[1,32,2560]{2,1,0:T(8,128)(2,1)S(1)}, u32[]{:S(2)}, u32[]{:S(2)}) collective-permute-start(bf16[1,32,2560]{2,1,0:T(8,128)(2,1)S(1)} %get-tuple-element.684), channel_id=1, source_target_pairs={{8,0},{16,8},{24,16},{9,1},{17,9},{25,17},{10,2},{18,10},{26,18},{... | collective-permute-start | bytes 491528 | tf_op jit(solution)/shard_map/while/body/eval_jaxpr/ppermute | solution.py:16
  43.7 7.7 %collective-permute-start = (bf16[1,32,2560]{2,1,0:T(8,128)(2,1)S(1)}, bf16[1,32,2560]{2,1,0:T(8,128)(2,1)S(1)}, u32[]{:S(2)}, u32[]{:S(2)}) collective-permute-start(bf16[1,32,2560]{2,1,0:T(8,128)(2,1)S(1)} %get-tuple-element.684), channel_id=1, source_target_pairs={{8,0},{16,8},{24,16},{9,1},{17,9},{25,17},{10,2},{18,10},{26,18},{... | collective-permute-start | bytes 491528 | tf_op jit(solution)/shard_map/while/body/eval_jaxpr/ppermute | solution.py:16
  51.4 43.8 %collective-permute-start = (bf16[1,32,2560]{2,1,0:T(8,128)(2,1)S(1)}, bf16[1,32,2560]{2,1,0:T(8,128)(2,1)S(1)}, u32[]{:S(2)}, u32[]{:S(2)}) collective-permute-start(bf16[1,32,2560]{2,1,0:T(8,128)(2,1)S(1)} %get-tuple-element.684), channel_id=1, source_target_pairs={{8,0},{16,8},{24,16},{9,1},{17,9},{25,17},{10,2},{18,10},{26,18},{... | collective-permute-start | bytes 491528 | tf_op jit(solution)/shard_map/while/body/eval_jaxpr/ppermute | solution.py:16
  107.8 7.2 %collective-permute-start = (bf16[1,32,2560]{2,1,0:T(8,128)(2,1)S(1)}, bf16[1,32,2560]{2,1,0:T(8,128)(2,1)S(1)}, u32[]{:S(2)}, u32[]{:S(2)}) collective-permute-start(bf16[1,32,2560]{2,1,0:T(8,128)(2,1)S(1)} %get-tuple-element.684), channel_id=1, source_target_pairs={{8,0},{16,8},{24,16},{9,1},{17,9},{25,17},{10,2},{18,10},{26,18},{... | collective-permute-start | bytes 491528 | tf_op jit(solution)/shard_map/while/body/eval_jaxpr/ppermute | solution.py:16
  127.6 7.2 %collective-permute-start = (bf16[1,32,2560]{2,1,0:T(8,128)(2,1)S(1)}, bf16[1,32,2560]{2,1,0:T(8,128)(2,1)S(1)}, u32[]{:S(2)}, u32[]{:S(2)}) collective-permute-start(bf16[1,32,2560]{2,1,0:T(8,128)(2,1)S(1)} %get-tuple-element.684), channel_id=1, source_target_pairs={{8,0},{16,8},{24,16},{9,1},{17,9},{25,17},{10,2},{18,10},{26,18},{... | collective-permute-start | bytes 491528 | tf_op jit(solution)/shard_map/while/body/eval_jaxpr/ppermute | solution.py:16
  147.4 7.2 %collective-permute-start = (bf16[1,32,2560]{2,1,0:T(8,128)(2,1)S(1)}, bf16[1,32,2560]{2,1,0:T(8,128)(2,1)S(1)}, u32[]{:S(2)}, u32[]{:S(2)}) collective-permute-start(bf16[1,32,2560]{2,1,0:T(8,128)(2,1)S(1)} %get-tuple-element.684), channel_id=1, source_target_pairs={{8,0},{16,8},{24,16},{9,1},{17,9},{25,17},{10,2},{18,10},{26,18},{... | collective-permute-start | bytes 491528 | tf_op jit(solution)/shard_map/while/body/eval_jaxpr/ppermute | solution.py:16
  167.2 7.2 %collective-permute-start = (bf16[1,32,2560]{2,1,0:T(8,128)(2,1)S(1)}, bf16[1,32,2560]{2,1,0:T(8,128)(2,1)S(1)}, u32[]{:S(2)}, u32[]{:S(2)}) collective-permute-start(bf16[1,32,2560]{2,1,0:T(8,128)(2,1)S(1)} %get-tuple-element.684), channel_id=1, source_target_pairs={{8,0},{16,8},{24,16},{9,1},{17,9},{25,17},{10,2},{18,10},{26,18},{... | collective-permute-start | bytes 491528 | tf_op jit(solution)/shard_map/while/body/eval_jaxpr/ppermute | solution.py:16
where the time goes:
time: 190 us; the launch traced here: 189 us
  waiting for transfers between devices  79.9 us (42%)
  matrix products  30.2 us (16%)
  other arithmetic  28.2 us (15%)
  local copies, waits for them, and re-layouts  24.2 us (13%)
  starting transfers between devices  14.2 us (7%)
  blocking collectives  10.2 us (5%)
    ppermute x7, waiting for transfers between devices, passed_along(): return lax.ppermute(block, axis, route)  79.9 us
    unnamed x1, other arithmetic  14.3 us
    all_gather x1, blocking collectives, shards(): maps_all = lax.all_gather(maps_here, 'dp', axis=1, tiled=True)  10.2 us
    dot_general x4, matrix products, block_back(): lax.dot_general(grad_bc, weights, (((1,), (1,)), ((), ())), preferred_ele...  9.94 us
    ppermute x7, starting transfers between devices, passed_along(): return lax.ppermute(block, axis, route)  9.04 us
    dot_general x4, matrix products, block_terms(): jnp.einsum('ihp,hpn->in', lead_grads, state_b, preferred_element_type=jnp...  5.47 us
    all_to_all x1, starting transfers between devices, shards(): rows_all = lax.all_to_all(rows_here, 'dp', 2, 1, tiled=True)  5.17 us
    unnamed x8, local copies, waits for them, and re-layouts  4 us
  transfers between devices with their start and end apart: 8, of which 7 were waited for; matrix products, arithmetic and copies ran while one was open for 32% of the time, Pallas kernels for 0%

commit v1 on v0

--- a/solution.py
+++ b/solution.py
@@ -176,7 +176,10 @@
     ways = lax.axis_size("dp")
     divisor = ways * seq_dev
     rows_here = layer_inputs.reshape(lay_dev, seq_dev * tok_len, features)
-    rows_all = lax.all_to_all(rows_here, "dp", 2, 1, tiled=True)
+    rows_all = jnp.concatenate(
+        lax.all_to_all(jnp.stack(jnp.split(rows_here, lax.psum(1, "dp"), axis=2)), "dp", 0, 0),
+        axis=1,
+    )
     maps_here = map_store.reshape(lay_dev, seq_dev * tok_len, map_store.shape[-1])
     maps_all = lax.all_gather(maps_here, "dp", axis=1, tiled=True)
     grad_w = (

time: 190 us -> 181 us (0.953)
  other arithmetic: 28.2 us -> 13.9 us
  local copies, waits for them, and re-layouts: 24.2 us -> 27.8 us
  waiting for transfers between devices: 79.9 us -> 82.4 us
    unnamed x1 -> x0, other arithmetic: 14.3 us -> none
    cond x0 -> x16, local copies, waits for them, and re-layouts: none -> 3.04 us
    reshape x1 -> x0, local copies, waits for them, and re-layouts: 2.51 us -> none  [shards(): rows_here = layer_inputs.reshape(lay_dev, seq_dev * tok_len, features)]
    ppermute x7, waiting for transfers between devices: 79.9 us -> 82.4 us  [passed_along(): return lax.ppermute(block, axis, route)]
    unnamed x8 -> x12, local copies, waits for them, and re-layouts: 4 us -> 5.94 us
  transfers between devices with their start and end apart: 8 -> 8, of which waited for: 7 -> 7; matrix products, arithmetic and copies ran while one was open for 32% -> 33% of each run, Pallas kernels for 0% -> 0%
where the time goes in v1:
time: 181 us; the launch traced here: 180 us
  waiting for transfers between devices  82.4 us (46%)
  matrix products  30.3 us (17%)
  local copies, waits for them, and re-layouts  27.8 us (15%)
  starting transfers between devices  14.2 us (8%)
  other arithmetic  13.9 us (8%)
  blocking collectives  9.7 us (5%)
    ppermute x7, waiting for transfers between devices, passed_along(): return lax.ppermute(block, axis, route)  82.4 us
    dot_general x4, matrix products, block_back(): lax.dot_general(grad_bc, weights, (((1,), (1,)), ((), ())), preferred_ele...  9.95 us
    all_gather x1, blocking collectives, shards(): maps_all = lax.all_gather(maps_here, 'dp', axis=1, tiled=True)  9.7 us
    ppermute x7, starting transfers between devices, passed_along(): return lax.ppermute(block, axis, route)  9 us
    unnamed x12, local copies, waits for them, and re-layouts  5.94 us
    dot_general x4, matrix products, block_terms(): jnp.einsum('ihp,hpn->in', lead_grads, state_b, preferred_element_type=jnp...  5.47 us
    all_to_all x1, starting transfers between devices, shards(): lax.all_to_all(jnp.stack(jnp.split(rows_here, lax.psum(1, 'dp'), axis=2))...  5.17 us
    convert_element_type x4, other arithmetic, block_terms(): (leading[:, :, None] * grads_b.astype(jnp.float32)).astype(jnp.bfloat16)  3.93 us
  transfers between devices with their start and end apart: 8, of which 7 were waited for; matrix products, arithmetic and copies ran while one was open for 33% of the time, Pallas kernels for 0%

profile of v1, /device:TPU:0, one launch (start us, length us, event | category | flops | bytes accessed | tf_op | source)
XLA Modules:
  0.0 179.7 jit_solution(12314841943728325290)
XLA Ops:
  0.6 1.4 copy.86
  7.1 5.2 %all-to-all-start = ((bf16[8,1,128,320]{2,3,1,0:T(8,128)(2,1)}), bf16[8,1,128,320]{2,3,1,0:T(8,128)(2,1)}, u32[]{:S(2)}, u32[]{:S(2)}) async-start(bf16[8,1,128,320]{2,3,1,0:T(8,128)(2,1)} %fusion.71), calls=%async_computation | async-start | bytes 1310720 | tf_op jit(solution)/shard_map/all_to_all | solution.py:180
  16.5 1.4 fusion.61
  19.5 1.9 %pad_maximum_fusion = bf16[1,1,4,40,64,128]{5,4,3,2,1,0:T(8,128)(2,1)} fusion(bf16[1,1,1,40,64,128]{5,4,3,2,1,0:T(8,128)(2,1)S(1)} %fusion.54, f32[1,1,1,40,64,128]{5,4,3,2,1,0:T(8,128)S(1)} %bitcast.202, f32[1,1,1,40,64,128]{5,4,3,2,1,0:T(8,128)S(1)} %bitcast.201, bf16[4]{0:T(256)(128)(2,1)S(1)} %pad.10.clone), kind=kLoop, calls=%fused_computation.78 | loop fusion | flops 3932160 | bytes 5898248 | tf_op jit(solution)/shard_map/vmap(vmap())/stack | solution.py:105
  22.5 144.9 %while.24 = (s32[]{:T(128)}, bf16[1,32,2560]{2,1,0:T(8,128)(2,1)S(1)}, f32[1,1,40,64,128]{4,3,2,1,0:T(8,128)S(1)}, bf16[1,1,128,2560]{3,2,1,0:T(8,128)(2,1)}, bf...) while((s32[]{:T(128)}, ...), condition=%wide.region_8.9_spmd, body=%wide.region_3.8_spmd.sunk | while | flops 140346368 | bytes 18077512 | solution.py:173
  23.9 7.4 %collective-permute-done = bf16[1,32,2560]{2,1,0:T(8,128)(2,1)S(1)} collective-permute-done((bf16[1,32,2560]{2,1,0:T(8,128)(2,1)S(1)}, bf16[1,32,2560]{2,1,0:T(8,128)(2,1)S(1)}, u32[]{:S(2)}, u32[]{:S(2)}) %collective-permute-start) | collective-permute-done | bytes 163872 | tf_op jit(solution)/shard_map/while/body/eval_jaxpr/ppermute | solution.py:16
  32.6 6.5 %collective-permute-done = bf16[1,32,2560]{2,1,0:T(8,128)(2,1)S(1)} collective-permute-done((bf16[1,32,2560]{2,1,0:T(8,128)(2,1)S(1)}, bf16[1,32,2560]{2,1,0:T(8,128)(2,1)S(1)}, u32[]{:S(2)}, u32[]{:S(2)}) %collective-permute-start) | collective-permute-done | bytes 163872 | tf_op jit(solution)/shard_map/while/body/eval_jaxpr/ppermute | solution.py:16
  40.5 44.9 %collective-permute-done = bf16[1,32,2560]{2,1,0:T(8,128)(2,1)S(1)} collective-permute-done((bf16[1,32,2560]{2,1,0:T(8,128)(2,1)S(1)}, bf16[1,32,2560]{2,1,0:T(8,128)(2,1)S(1)}, u32[]{:S(2)}, u32[]{:S(2)}) %collective-permute-start) | collective-permute-done | bytes 163872 | tf_op jit(solution)/shard_map/while/body/eval_jaxpr/ppermute | solution.py:16
  85.3 13.3 %conditional.2 = (bf16[1,32,2560]{2,1,0:T(8,128)(2,1)S(1)}, f32[1,1,40,64,128]{4,3,2,1,0:T(8,128)S(1)}, bf16[1,1,128,2560]{3,2,1,0:T(8,128)(2,1)}, bf16[1,1,128,256]{3,2,1,0:T(8,128)(2,1)S(1)}) conditional(s32[]{:T(128)} %convert_element_type.236, (f32[1,1,40,64,128]{4,3,2,1,0:T(8,128)S(1)}, bf16[1,1,128,2560]{3,2,1,0:T(8,128)(2,1)}, ...), branch_computations={%region_4.4_spmd, %region_5.7_spmd} | conditional | flops 140346368 | bytes 17421804 | solution.py:159
  91.4 1.4 fusion.13
  95.3 2.5 %bitcast_dynamic-update-slice_fusion = (bf16[1,1,128,2560]{3,2,1,0:T(8,128)(2,1)}, bf16[1,32,2560]{2,1,0:T(8,128)(2,1)S(1)}) fusion(bf16[1,1,128,2560]{3,2,1,0:T(8,128)(2,1)} %get-tuple-element.483, s32[]{:T(128)S(6)} %select_n.90, bf16[1,2560,256]{2,1,0:T(8,128)(2,1)} %get-tuple-element.482, bf16[32,128]{1,0:T(8,128)(2,1)S(1)} %fusion.13, ...), kind=kOutput, calls=%fused_computation.46 | convolution fusion | flops 42303488 | bytes 2146308 | tf_op jit(solution)/shard_map/while/body/eval_jaxpr/cond/branch_1_fun/vmap()/dot_general | solution.py:84
  99.9 5.9 %collective-permute-done = bf16[1,32,2560]{2,1,0:T(8,128)(2,1)S(1)} collective-permute-done((bf16[1,32,2560]{2,1,0:T(8,128)(2,1)S(1)}, bf16[1,32,2560]{2,1,0:T(8,128)(2,1)S(1)}, u32[]{:S(2)}, u32[]{:S(2)}) %collective-permute-start) | collective-permute-done | bytes 163872 | tf_op jit(solution)/shard_map/while/body/eval_jaxpr/ppermute | solution.py:16
  105.9 13.3 %conditional.2 = (bf16[1,32,2560]{2,1,0:T(8,128)(2,1)S(1)}, f32[1,1,40,64,128]{4,3,2,1,0:T(8,128)S(1)}, bf16[1,1,128,2560]{3,2,1,0:T(8,128)(2,1)}, bf16[1,1,128,256]{3,2,1,0:T(8,128)(2,1)S(1)}) conditional(s32[]{:T(128)} %convert_element_type.236, (f32[1,1,40,64,128]{4,3,2,1,0:T(8,128)S(1)}, bf16[1,1,128,2560]{3,2,1,0:T(8,128)(2,1)}, ...), branch_computations={%region_4.4_spmd, %region_5.7_spmd} | conditional | flops 140346368 | bytes 17421804 | solution.py:159
  115.8 2.5 %bitcast_dynamic-update-slice_fusion = (bf16[1,1,128,2560]{3,2,1,0:T(8,128)(2,1)}, bf16[1,32,2560]{2,1,0:T(8,128)(2,1)S(1)}) fusion(bf16[1,1,128,2560]{3,2,1,0:T(8,128)(2,1)} %get-tuple-element.483, s32[]{:T(128)S(6)} %select_n.90, bf16[1,2560,256]{2,1,0:T(8,128)(2,1)} %get-tuple-element.482, bf16[32,128]{1,0:T(8,128)(2,1)S(1)} %fusion.13, ...), kind=kOutput, calls=%fused_computation.46 | convolution fusion | flops 42303488 | bytes 2146308 | tf_op jit(solution)/shard_map/while/body/eval_jaxpr/cond/branch_1_fun/vmap()/dot_general | solution.py:84
  120.5 5.9 %collective-permute-done = bf16[1,32,2560]{2,1,0:T(8,128)(2,1)S(1)} collective-permute-done((bf16[1,32,2560]{2,1,0:T(8,128)(2,1)S(1)}, bf16[1,32,2560]{2,1,0:T(8,128)(2,1)S(1)}, u32[]{:S(2)}, u32[]{:S(2)}) %collective-permute-start) | collective-permute-done | bytes 163872 | tf_op jit(solution)/shard_map/while/body/eval_jaxpr/ppermute | solution.py:16
  126.4 13.3 %conditional.2 = (bf16[1,32,2560]{2,1,0:T(8,128)(2,1)S(1)}, f32[1,1,40,64,128]{4,3,2,1,0:T(8,128)S(1)}, bf16[1,1,128,2560]{3,2,1,0:T(8,128)(2,1)}, bf16[1,1,128,256]{3,2,1,0:T(8,128)(2,1)S(1)}) conditional(s32[]{:T(128)} %convert_element_type.236, (f32[1,1,40,64,128]{4,3,2,1,0:T(8,128)S(1)}, bf16[1,1,128,2560]{3,2,1,0:T(8,128)(2,1)}, ...), branch_computations={%region_4.4_spmd, %region_5.7_spmd} | conditional | flops 140346368 | bytes 17421804 | solution.py:159
  136.4 2.5 %bitcast_dynamic-update-slice_fusion = (bf16[1,1,128,2560]{3,2,1,0:T(8,128)(2,1)}, bf16[1,32,2560]{2,1,0:T(8,128)(2,1)S(1)}) fusion(bf16[1,1,128,2560]{3,2,1,0:T(8,128)(2,1)} %get-tuple-element.483, s32[]{:T(128)S(6)} %select_n.90, bf16[1,2560,256]{2,1,0:T(8,128)(2,1)} %get-tuple-element.482, bf16[32,128]{1,0:T(8,128)(2,1)S(1)} %fusion.13, ...), kind=kOutput, calls=%fused_computation.46 | convolution fusion | flops 42303488 | bytes 2146308 | tf_op jit(solution)/shard_map/while/body/eval_jaxpr/cond/branch_1_fun/vmap()/dot_general | solution.py:84
  141.0 5.9 %collective-permute-done = bf16[1,32,2560]{2,1,0:T(8,128)(2,1)S(1)} collective-permute-done((bf16[1,32,2560]{2,1,0:T(8,128)(2,1)S(1)}, bf16[1,32,2560]{2,1,0:T(8,128)(2,1)S(1)}, u32[]{:S(2)}, u32[]{:S(2)}) %collective-permute-start) | collective-permute-done | bytes 163872 | tf_op jit(solution)/shard_map/while/body/eval_jaxpr/ppermute | solution.py:16
  146.9 13.3 %conditional.2 = (bf16[1,32,2560]{2,1,0:T(8,128)(2,1)S(1)}, f32[1,1,40,64,128]{4,3,2,1,0:T(8,128)S(1)}, bf16[1,1,128,2560]{3,2,1,0:T(8,128)(2,1)}, bf16[1,1,128,256]{3,2,1,0:T(8,128)(2,1)S(1)}) conditional(s32[]{:T(128)} %convert_element_type.236, (f32[1,1,40,64,128]{4,3,2,1,0:T(8,128)S(1)}, bf16[1,1,128,2560]{3,2,1,0:T(8,128)(2,1)}, ...), branch_computations={%region_4.4_spmd, %region_5.7_spmd} | conditional | flops 140346368 | bytes 17421804 | solution.py:159
  153.0 1.4 fusion.13
  156.9 2.5 %bitcast_dynamic-update-slice_fusion = (bf16[1,1,128,2560]{3,2,1,0:T(8,128)(2,1)}, bf16[1,32,2560]{2,1,0:T(8,128)(2,1)S(1)}) fusion(bf16[1,1,128,2560]{3,2,1,0:T(8,128)(2,1)} %get-tuple-element.483, s32[]{:T(128)S(6)} %select_n.90, bf16[1,2560,256]{2,1,0:T(8,128)(2,1)} %get-tuple-element.482, bf16[32,128]{1,0:T(8,128)(2,1)S(1)} %fusion.13, ...), kind=kOutput, calls=%fused_computation.46 | convolution fusion | flops 42303488 | bytes 2146308 | tf_op jit(solution)/shard_map/while/body/eval_jaxpr/cond/branch_1_fun/vmap()/dot_general | solution.py:84
  161.5 5.9 %collective-permute-done = bf16[1,32,2560]{2,1,0:T(8,128)(2,1)S(1)} collective-permute-done((bf16[1,32,2560]{2,1,0:T(8,128)(2,1)S(1)}, bf16[1,32,2560]{2,1,0:T(8,128)(2,1)S(1)}, u32[]{:S(2)}, u32[]{:S(2)}) %collective-permute-start) | collective-permute-done | bytes 163872 | tf_op jit(solution)/shard_map/while/body/eval_jaxpr/ppermute | solution.py:16
  167.4 9.7 %all-gather = bf16[1,1,1024,256]{3,2,1,0:T(8,128)(2,1)S(1)} all-gather(bf16[1,1,128,256]{3,2,1,0:T(8,128)(2,1)S(1)} %get-tuple-element.508), channel_id=2, replica_groups=mesh['section'=4,'dp'=8] {'dp'}, dimensions={2}, use_global_device_ids=true | all-gather | bytes 589824 | tf_op jit(solution)/shard_map/all_gather | solution.py:184
  177.1 1.5 copy.87
  (204 shorter events, 62.1 us)
Async XLA Ops:
  2.0 10.3 %copy-start.1 = (f32[1,1,128,40]{2,3,1,0:T(8,128)S(1)}, f32[1,1,128,40]{2,3,1,0:T(8,128)}, u32[]{:S(2)}) copy-start(f32[1,1,128,40]{2,3,1,0:T(8,128)} %param.16) | copy-start | bytes 61444
  7.1 170.0 %all-to-all-start = ((bf16[8,1,128,320]{2,3,1,0:T(8,128)(2,1)}), bf16[8,1,128,320]{2,3,1,0:T(8,128)(2,1)}, u32[]{:S(2)}, u32[]{:S(2)}) async-start(bf16[8,1,128,320]{2,3,1,0:T(8,128)(2,1)} %fusion.71), calls=%async_computation | async-start | bytes 1310720 | tf_op jit(solution)/shard_map/all_to_all | solution.py:180
  14.9 1.6 copy-start
  22.6 8.7 %collective-permute-start = (bf16[1,32,2560]{2,1,0:T(8,128)(2,1)S(1)}, bf16[1,32,2560]{2,1,0:T(8,128)(2,1)S(1)}, u32[]{:S(2)}, u32[]{:S(2)}) collective-permute-start(bf16[1,32,2560]{2,1,0:T(8,128)(2,1)S(1)} %get-tuple-element.684), channel_id=1, source_target_pairs={{8,0},{16,8},{24,16},{9,1},{17,9},{25,17},{10,2},{18,10},{26,18},{... | collective-permute-start | bytes 491528 | tf_op jit(solution)/shard_map/while/body/eval_jaxpr/ppermute | solution.py:16
  31.3 7.8 %collective-permute-start = (bf16[1,32,2560]{2,1,0:T(8,128)(2,1)S(1)}, bf16[1,32,2560]{2,1,0:T(8,128)(2,1)S(1)}, u32[]{:S(2)}, u32[]{:S(2)}) collective-permute-start(bf16[1,32,2560]{2,1,0:T(8,128)(2,1)S(1)} %get-tuple-element.684), channel_id=1, source_target_pairs={{8,0},{16,8},{24,16},{9,1},{17,9},{25,17},{10,2},{18,10},{26,18},{... | collective-permute-start | bytes 491528 | tf_op jit(solution)/shard_map/while/body/eval_jaxpr/ppermute | solution.py:16
  39.2 46.2 %collective-permute-start = (bf16[1,32,2560]{2,1,0:T(8,128)(2,1)S(1)}, bf16[1,32,2560]{2,1,0:T(8,128)(2,1)S(1)}, u32[]{:S(2)}, u32[]{:S(2)}) collective-permute-start(bf16[1,32,2560]{2,1,0:T(8,128)(2,1)S(1)} %get-tuple-element.684), channel_id=1, source_target_pairs={{8,0},{16,8},{24,16},{9,1},{17,9},{25,17},{10,2},{18,10},{26,18},{... | collective-permute-start | bytes 491528 | tf_op jit(solution)/shard_map/while/body/eval_jaxpr/ppermute | solution.py:16
  85.3 0.6 copy-start.2
  97.8 0.8 copy-start.3
  98.7 7.2 %collective-permute-start = (bf16[1,32,2560]{2,1,0:T(8,128)(2,1)S(1)}, bf16[1,32,2560]{2,1,0:T(8,128)(2,1)S(1)}, u32[]{:S(2)}, u32[]{:S(2)}) collective-permute-start(bf16[1,32,2560]{2,1,0:T(8,128)(2,1)S(1)} %get-tuple-element.684), channel_id=1, source_target_pairs={{8,0},{16,8},{24,16},{9,1},{17,9},{25,17},{10,2},{18,10},{26,18},{... | collective-permute-start | bytes 491528 | tf_op jit(solution)/shard_map/while/body/eval_jaxpr/ppermute | solution.py:16
  105.9 0.6 copy-start.2
  118.3 0.8 copy-start.3
  119.2 7.2 %collective-permute-start = (bf16[1,32,2560]{2,1,0:T(8,128)(2,1)S(1)}, bf16[1,32,2560]{2,1,0:T(8,128)(2,1)S(1)}, u32[]{:S(2)}, u32[]{:S(2)}) collective-permute-start(bf16[1,32,2560]{2,1,0:T(8,128)(2,1)S(1)} %get-tuple-element.684), channel_id=1, source_target_pairs={{8,0},{16,8},{24,16},{9,1},{17,9},{25,17},{10,2},{18,10},{26,18},{... | collective-permute-start | bytes 491528 | tf_op jit(solution)/shard_map/while/body/eval_jaxpr/ppermute | solution.py:16
  126.4 0.6 copy-start.2
  138.9 0.8 copy-start.3
  139.7 7.2 %collective-permute-start = (bf16[1,32,2560]{2,1,0:T(8,128)(2,1)S(1)}, bf16[1,32,2560]{2,1,0:T(8,128)(2,1)S(1)}, u32[]{:S(2)}, u32[]{:S(2)}) collective-permute-start(bf16[1,32,2560]{2,1,0:T(8,128)(2,1)S(1)} %get-tuple-element.684), channel_id=1, source_target_pairs={{8,0},{16,8},{24,16},{9,1},{17,9},{25,17},{10,2},{18,10},{26,18},{... | collective-permute-start | bytes 491528 | tf_op jit(solution)/shard_map/while/body/eval_jaxpr/ppermute | solution.py:16
  146.9 0.6 copy-start.2
  159.4 0.8 copy-start.3
  160.2 7.2 %collective-permute-start = (bf16[1,32,2560]{2,1,0:T(8,128)(2,1)S(1)}, bf16[1,32,2560]{2,1,0:T(8,128)(2,1)S(1)}, u32[]{:S(2)}, u32[]{:S(2)}) collective-permute-start(bf16[1,32,2560]{2,1,0:T(8,128)(2,1)S(1)} %get-tuple-element.684), channel_id=1, source_target_pairs={{8,0},{16,8},{24,16},{9,1},{17,9},{25,17},{10,2},{18,10},{26,18},{... | collective-permute-start | bytes 491528 | tf_op jit(solution)/shard_map/while/body/eval_jaxpr/ppermute | solution.py:16
